TPU v7x, 128 devices: a whole 4x4x4 slice. The times are simulated.
128 devices in a mesh: shard: 8 (over y, core), tensor: 4 (over z), section: 4 (over x).
Axes of the slice: x: 4, y: 4, z: 4, core: 2. Of those that a mesh axis runs over, the one named last changes fastest.
Arguments:
- activations: bfloat16 [4, 16384, 2048], P('section', 'shard'), may hold values from -500 to 500, as said below
- out_grad: bfloat16 [4, 16384, 8192], P('section', 'shard', 'tensor'), may hold values from -30 to 30, as said below
- basis: float32 [4, 2048, 256], P('section', 'shard'), may hold values from -0.125 to 0.125
- first_moment: float32 [4, 256, 8192], P('section', 'shard', 'tensor'), may hold values from -6 to 6
- second_moment: float32 [4, 256, 8192], P('section', 'shard', 'tensor'), may hold values from 0.5 to 2
- gain_partial: float32 [4, 8, 2048], P('section', 'shard'), may hold values from -4096 to 4096
- gain_first: float32 [4, 2048], P('section', 'shard'), may hold values from -6 to 6
- gain_second: float32 [4, 2048], P('section', 'shard'), may hold values from 0.5 to 2
Outputs:
- update: float32 [4, 2048, 8192], P('section', 'shard', 'tensor')
- first_out: float32 [4, 256, 8192], P('section', 'shard', 'tensor')
- second_out: float32 [4, 256, 8192], P('section', 'shard', 'tensor')
- new_basis: float32 [4, 2048, 256], P('section', ('shard', 'tensor'))
- gain_step: float32 [4, 2048], P('section', 'shard')
- gain_first_out: float32 [4, 2048], P('section', 'shard')
- gain_second_out: float32 [4, 2048], P('section', 'shard')
Inputs may be any that keep to these rules, and one draw needn't show every extreme that they name: Real-valued activations whose column scales differ from column to column. `out_grad`: Real-valued gradients whose column scales differ from column to column.
All inputs are finite; a program needn't handle non-finite values.
Results may differ from a plain program's by a relative error of at most 0.0003.
Values sent between devices are 32-bit elements; how exact they have to be, the bound alone decides.
No kernel may reach another device: no remote copies, remote signals or barrier semaphores. Data moves between devices by JAX's collectives and lax.ppermute only.
A program may use at most 128 MiB of HBM per device.

v0:
```python
import jax
import jax.numpy as jnp
from jax import lax
from jax.sharding import PartitionSpec as P

D = 2048
FF = 8192
NS_STEPS = 5
STEP = 8
exact_mode = lax.Precision.HIGHEST
beta_one = 0.9
beta_two = 0.999
adam_eps = 1e-08
clip_eps = 1e-06
ns_eps = 1e-07
coef_first = 3.4445
coef_second = -4.775
coef_third = 2.0315


def adam_direction(clipped, first_old, second_old):
    first_new = beta_one * first_old + (1.0 - beta_one) * clipped
    second_new = beta_two * second_old + (1.0 - beta_two) * clipped * clipped
    direction = (
        first_new
        / (1.0 - beta_one**STEP)
        / (jnp.sqrt(second_new / (1.0 - beta_two**STEP)) + adam_eps)
    )
    return (first_new, second_new, direction)


def ns_update(current, gram):
    mixer = coef_second * gram + coef_third * jnp.dot(gram, gram, precision=exact_mode)
    return coef_first * current + jnp.dot(current, mixer, precision=exact_mode)


def gram_of(block):
    local_gram = jnp.dot(block.T, block, precision=exact_mode)
    return lax.psum(local_gram, ("shard", "tensor"))


def shards(
    activations, out_grad, basis, first_moment, second_moment, gain_partial, gain_first, gain_second
):
    tensors = lax.axis_size("tensor")
    shard_pos = lax.axis_index("shard")
    layer_count = activations.shape[0]
    rows_here = basis.shape[1]
    rank_rows = first_moment.shape[1]
    cols_here = out_grad.shape[2]
    layer_index = 0
    tokens_in = activations[layer_index]
    grads_out = out_grad[layer_index]
    basis_here = basis[layer_index]

    def row_term(start, count, tokens_in=tokens_in, grads_out=grads_out):
        return lax.dot_general(
            tokens_in, grads_out, (((0,), (0,)), ((), ())), preferred_element_type=jnp.float32
        )

    grad_block = lax.psum_scatter(
        row_term(jnp.int32(0), lax.axis_size("shard") * rows_here),
        "shard",
        scatter_dimension=0,
        tiled=True,
    )
    part_proj = jnp.dot(basis_here.T, grad_block, precision=exact_mode)
    proj_full, gain_total = lax.psum((part_proj, gain_partial[layer_index, 0]), "shard")
    proj_rows = lax.dynamic_slice_in_dim(proj_full, shard_pos * rank_rows, rank_rows, 0)
    square_sum = jnp.sum(grad_block * grad_block)

    def refresh_term(start, count, grad_block=grad_block, proj_full=proj_full):
        return lax.dot_general(
            grad_block, proj_full, (((1,), (1,)), ((), ())), precision=exact_mode
        )

    refreshed = lax.psum_scatter(
        refresh_term(jnp.int32(0), lax.axis_size("tensor") * (rows_here // tensors)),
        "tensor",
        scatter_dimension=0,
        tiled=True,
    )
    kept_list = [basis_here]
    gain_own = lax.dynamic_slice_in_dim(gain_total, shard_pos * rows_here, rows_here, 0)
    square_sum = square_sum + jnp.sum(gain_own * gain_own) / float(tensors)
    proj_list = [proj_rows]
    gain_list = [gain_own]
    refresh_list = [refreshed]
    total_sq = lax.psum(square_sum, ("shard", "tensor", "section"))
    entry_count = float(lax.axis_size("section") * layer_count * (D * FF + D))
    clip = jnp.minimum(1.0, lax.rsqrt(total_sq / entry_count + clip_eps))
    layer_index = 0
    first_new, second_new, direction = adam_direction(
        clip * proj_list[layer_index], first_moment[layer_index], second_moment[layer_index]
    )
    firsts = [first_new]
    seconds = [second_new]
    kept_basis = kept_list[layer_index]

    def fold_rows(total, piece, start, kept_basis=kept_basis):
        return jnp.dot(kept_basis, piece, precision=exact_mode)

    empty = jnp.zeros((rows_here, cols_here), jnp.float32)
    update_here = fold_rows(
        empty, lax.all_gather(direction, "shard", axis=0, tiled=True), jnp.int32(0)
    )
    updates = [update_here]
    refreshed = refresh_list[layer_index]
    frob = lax.psum(jnp.sum(refreshed * refreshed), ("shard", "tensor"))
    current = refreshed / jnp.sqrt(frob + ns_eps)
    gram = gram_of(current)
    for step_index in range(NS_STEPS):
        current = ns_update(current, gram)
        if step_index + 1 < NS_STEPS:
            gram = gram_of(current)
    bases = [current]
    gain_first_new, gain_second_new, gain_dir = adam_direction(
        clip * gain_list[layer_index], gain_first[layer_index], gain_second[layer_index]
    )
    gain_steps = [gain_dir]
    gain_firsts = [gain_first_new]
    gain_seconds = [gain_second_new]
    return (
        jnp.stack(updates),
        jnp.stack(firsts),
        jnp.stack(seconds),
        jnp.stack(bases),
        jnp.stack(gain_steps),
        jnp.stack(gain_firsts),
        jnp.stack(gain_seconds),
    )


def solution(mesh):
    placed = (
        P("section", "shard", None),
        P("section", "shard", "tensor"),
        P("section", "shard", None),
        P("section", "shard", "tensor"),
        P("section", "shard", "tensor"),
        P("section", "shard", None),
        P("section", "shard"),
        P("section", "shard"),
    )
    return jax.shard_map(
        shards,
        mesh=mesh,
        in_specs=placed,
        out_specs=(
            P("section", "shard", "tensor"),
            P("section", "shard", "tensor"),
            P("section", "shard", "tensor"),
            P("section", ("shard", "tensor"), None),
            P("section", "shard"),
            P("section", "shard"),
            P("section", "shard"),
        ),
        check_vma=False,
    )
```

profile of v0, /device:TPU:1, one launch (start us, length us, event | category | flops | bytes accessed | tf_op | source)
XLA Modules:
  0.0 854.7 jit_solution(13370359571268590590)
XLA Ops:
  7.2 24.3 %fusion = f32[2048,2048]{1,0:T(8,128)} fusion(bf16[1,2048,2048]{2,1,0:T(8,128)(2,1)} %param.9, bf16[1,2048,2048]{2,1,0:T(8,128)(2,1)} %param.8), kind=kOutput, calls=%fused_computation | convolution fusion | flops 17179869184 | bytes 33554432 | tf_op jit(solution)/shard_map/dot_general | solution.py:57
  31.6 94.5 %reduce-scatter.3.cloned.1.call-done = f32[256,2048]{1,0:T(8,128)} async-done(((f32[2048,2048]{1,0:T(8,128)}), f32[256,2048]{1,0:T(8,128)}) %reduce-scatter.3.cloned.1.call-update) | async-done | bytes 2097168 | tf_op jit(solution)/shard_map/reduce_scatter | solution.py:61
  126.1 6.4 convolution_bitcast_fusion.1
  132.6 64.0 %all-reduce.7.cloned.1.call-done = f32[256,2048]{0,1:T(8,128)} async-done(((f32[256,2048]{0,1:T(8,128)}), f32[256,2048]{0,1:T(8,128)}) %all-reduce.7.cloned.1.call-update) | async-done | bytes 2097168 | tf_op jit(solution)/shard_map/psum | solution.py:68
  196.6 4.2 fusion.17
  200.9 20.4 %reduce-scatter.5.cloned.1.call-done = f32[64,256]{1,0:T(8,128)} async-done(((f32[256,256]{1,0:T(8,128)}), f32[64,256]{1,0:T(8,128)}) %reduce-scatter.5.cloned.1.call-update) | async-done | bytes 65552 | tf_op jit(solution)/shard_map/reduce_scatter | solution.py:77
  221.2 1.5 multiply_reduce_fusion.1
  222.7 62.0 %psum.66 = f32[]{:T(128)} all-reduce(f32[]{:T(128)} %multiply_reduce_fusion.1), channel_id=1, replica_groups=mesh['shard'=8,'tensor'=4,'section'=4] {'shard','tensor'}, use_global_device_ids=true, to_apply=%region_8.0 | all-reduce | flops 1 | bytes 8 | tf_op jit(solution)/shard_map/psum | solution.py:109
  285.4 2.0 fusion.14
  287.5 104.3 %all-reduce.9.cloned.1.call-done = f32[256,256]{1,0:T(8,128)} async-done(((f32[256,256]{1,0:T(8,128)}), f32[256,256]{1,0:T(8,128)}) %all-reduce.9.cloned.1.call-update) | async-done | bytes 262160 | tf_op jit(solution)/shard_map/psum | solution.py:39
  391.8 1.5 fusion.7
  393.3 1.2 convolution_add_fusion.4
  395.8 101.9 %all-reduce.11.cloned.1.call-done = f32[256,256]{1,0:T(8,128)} async-done(((f32[256,256]{1,0:T(8,128)}), f32[256,256]{1,0:T(8,128)}) %all-reduce.11.cloned.1.call-update) | async-done | bytes 262160 | tf_op jit(solution)/shard_map/psum | solution.py:39
  497.7 1.5 fusion.6
  499.4 1.1 fusion.19
  500.7 1.3 copy.20
  501.9 2.3 copy.21
  504.2 13.5 %psum.63 = f32[2048]{0:T(1024)S(1)} all-reduce(f32[2048]{0:T(1024)S(1)} %bitcast.72), channel_id=1, replica_groups=mesh['shard'=8,'tensor'=4,'section'=4] {'shard'}, use_global_device_ids=true, to_apply=%region_2.0 | all-reduce | flops 2048 | bytes 16384 | tf_op jit(solution)/shard_map/psum | solution.py:68
  519.0 84.3 %all-reduce.13.cloned.1.call-done = f32[256,256]{1,0:T(8,128)} async-done(((f32[256,256]{1,0:T(8,128)}), f32[256,256]{1,0:T(8,128)}) %all-reduce.13.cloned.1.call-update) | async-done | bytes 262160 | tf_op jit(solution)/shard_map/psum | solution.py:39
  603.3 1.5 fusion.5
  606.3 1.1 multiply_reduce_fusion
  608.2 65.9 %psum.64 = f32[]{:T(128)} all-reduce(f32[]{:T(128)S(6)} %add.92), channel_id=1, replica_groups=mesh['shard'=8,'tensor'=4,'section'=4] {'shard','tensor','section'}, use_global_device_ids=true, to_apply=%region_4.0 | all-reduce | flops 1 | bytes 8 | tf_op jit(solution)/shard_map/psum | solution.py:89
  674.7 34.5 %all-reduce.15.cloned.1.call-done = f32[256,256]{1,0:T(8,128)} async-done(((f32[256,256]{1,0:T(8,128)}), f32[256,256]{1,0:T(8,128)}) %all-reduce.15.cloned.1.call-update) | async-done | bytes 262160 | tf_op jit(solution)/shard_map/psum | solution.py:39
  709.2 1.5 fusion.4
  711.0 1.1 fusion.21
  712.2 3.3 fusion.13
  715.5 2.3 copy.22
  720.6 93.8 %all-reduce.17.cloned.1.call-done = f32[256,256]{1,0:T(8,128)} async-done(((f32[256,256]{1,0:T(8,128)}), f32[256,256]{1,0:T(8,128)}) %all-reduce.17.cloned.1.call-update) | async-done | bytes 262160 | tf_op jit(solution)/shard_map/psum | solution.py:39
  814.4 1.5 fusion.3
  816.9 24.5 %all-gather.2.cloned.1.call-done = f32[256,2048]{1,0:T(8,128)} async-done(((f32[32,2048]{1,0:T(8,128)}), f32[256,2048]{1,0:T(8,128)}) %all-gather.2.cloned.1.call-update) | async-done | bytes 2097168 | tf_op jit(solution)/shard_map/all_gather | solution.py:105
  841.4 5.0 convolution_bitcast_fusion
  846.4 1.8 copy.23
  (44 shorter events, 8.0 us)
Async XLA Ops:
  7.2 119.0 %copy-start = (f32[1,256,256]{2,1,0:T(8,128)S(1)}, f32[1,256,256]{2,1,0:T(8,128)}, u32[]{:S(2)}) copy-start(f32[1,256,256]{2,1,0:T(8,128)} %param.10) | copy-start | bytes 786436
  7.2 119.0 %reduce-scatter.3.cloned.1.call-start = ((), (), s32[]{:S(2)}) async-start(), calls=%async_computation.2 | async-start | bytes 18874368 | tf_op jit(solution)/shard_map/reduce_scatter | solution.py:61
  31.5 165.1 %all-reduce.7.cloned.1.call-start = ((), (), s32[]{:S(2)}) async-start(), calls=%async_computation.3 | async-start | bytes 4194304 | tf_op jit(solution)/shard_map/psum | solution.py:68
  132.5 64.1 %copy-start.1 = (f32[256,2048]{1,0:T(8,128)S(1)}, f32[256,2048]{1,0:T(8,128)}, u32[]{:S(2)}) copy-start(f32[256,2048]{1,0:T(8,128)} %reduce-scatter.3.cloned.1.call-done) | copy-start | bytes 6291460
  132.5 88.7 %reduce-scatter.5.cloned.1.call-start = ((), (), s32[]{:S(2)}) async-start(), calls=%async_computation.5 | async-start | bytes 327680 | tf_op jit(solution)/shard_map/reduce_scatter | solution.py:77
  200.8 191.0 %all-reduce.9.cloned.1.call-start = ((), (), s32[]{:S(2)}) async-start(), calls=%async_computation.6 | async-start | bytes 524288 | tf_op jit(solution)/shard_map/psum | solution.py:39
  287.4 210.3 %all-reduce.11.cloned.1.call-start = ((), (), s32[]{:S(2)}) async-start(), calls=%async_computation.7 | async-start | bytes 524288 | tf_op jit(solution)/shard_map/psum | solution.py:39
  395.6 108.6 %copy-start.4 = (f32[1,1,2048]{2,1,0:T(1,128)S(1)}, f32[1,1,2048]{2,1,0:T(1,128)}, u32[]{:S(2)}) copy-start(f32[1,1,2048]{2,1,0:T(1,128)} %param.13) | copy-start | bytes 24580
  395.6 207.8 %all-reduce.13.cloned.1.call-start = ((), (), s32[]{:S(2)}) async-start(), calls=%async_computation.8 | async-start | bytes 524288 | tf_op jit(solution)/shard_map/psum | solution.py:39
  500.6 208.6 %all-reduce.15.cloned.1.call-start = ((), (), s32[]{:S(2)}) async-start(), calls=%async_computation.9 | async-start | bytes 524288 | tf_op jit(solution)/shard_map/psum | solution.py:39
  606.2 208.2 %all-reduce.17.cloned.1.call-start = ((), (), s32[]{:S(2)}) async-start(), calls=%async_computation.10 | async-start | bytes 524288 | tf_op jit(solution)/shard_map/psum | solution.py:39
  607.4 104.8 %copy-start.2 = (f32[1,32,2048]{1,2,0:T(8,128)S(1)}, f32[1,32,2048]{1,2,0:T(8,128)}, u32[]{:S(2)}) copy-start(f32[1,32,2048]{1,2,0:T(8,128)} %copy.21) | copy-start | bytes 786436
  712.1 5.7 copy-start.5
  712.1 5.8 copy-start.6
  712.1 129.2 %all-gather.2.cloned.1.call-start = ((), (), s32[]{:S(2)}) async-start(), calls=%async_computation.4 | async-start | bytes 2359296 | tf_op jit(solution)/shard_map/all_gather | solution.py:105
  715.5 3.1 copy-start.3
Sparse Core Ops, SparseCore 0:
  31.7 94.4 reduce-scatter.2
  132.6 63.9 all-reduce.6
  200.9 20.2 reduce-scatter.4
  287.6 104.1 all-reduce.8
  395.7 101.9 all-reduce.10
  501.4 101.9 all-reduce.12
  607.1 102.0 all-reduce.14
  712.4 101.9 all-reduce.16
  816.2 25.1 all-gather.1
where the time goes:
time: 855 us
  waiting for transfers between devices  622 us (73%)
  blocking collectives  141 us (16%)
  matrix products  56.7 us (7%)
  between operations  16.8 us (2%)
  local copies, waits for them, and re-layouts  9.74 us (1%)
    psum x5, waiting for transfers between devices, gram_of(): return lax.psum(local_gram, ('shard', 'tensor'))  419 us
    reduce_scatter x1, waiting for transfers between devices, shards(): lax.psum_scatter(row_term(jnp.int32(0), lax.axis_size('shard') * rows_her...  94.5 us
    psum x1, blocking collectives, shards(): total_sq = lax.psum(square_sum, ('shard', 'tensor', 'section'))  65.9 us
    psum x1, waiting for transfers between devices, shards(): lax.psum((part_proj, gain_partial[layer_index, 0]), 'shard')  64 us
    psum x1, blocking collectives, shards(): frob = lax.psum(jnp.sum(refreshed * refreshed), ('shard', 'tensor'))  62 us
    all_gather x1, waiting for transfers between devices, shards(): lax.all_gather(direction, 'shard', axis=0, tiled=True)  24.5 us
    dot_general x1, matrix products, row_term(): lax.dot_general(tokens_in, grads_out, (((0,), (0,)), ((), ())), preferred...  24.3 us
    reduce_scatter x1, waiting for transfers between devices, shards(): lax.psum_scatter(refresh_term(jnp.int32(0), lax.axis_size('tensor') * (ro...  20.4 us
  transfers between devices with their start and end apart: 9, of which 9 were waited for; matrix products, arithmetic and copies ran while one was open for 2% of the time, Pallas kernels for 0%

commit v1 on v0

--- a/solution.py
+++ b/solution.py
@@ -36,7 +36,7 @@
 
 def gram_of(block):
     local_gram = jnp.dot(block.T, block, precision=exact_mode)
-    return lax.psum(local_gram, ("shard", "tensor"))
+    return jnp.sum(lax.all_gather(local_gram, ("shard", "tensor")), axis=0)
 
 
 def shards(

time: 855 us -> 648 us (0.76)
  waiting for transfers between devices: 622 us -> 402 us
  other arithmetic: 7.26 us -> 26.9 us
    psum x5 -> x0, waiting for transfers between devices: 419 us -> none  [gram_of(): return lax.psum(local_gram, ('shard', 'tensor'))]
    all_gather x0 -> x5, waiting for transfers between devices: none -> 209 us  [gram_of(): return jnp.sum(lax.all_gather(local_gram, ('shard', 'tensor')), axis=0)]
    reduce_sum x0 -> x5, other arithmetic: none -> 19.7 us  [gram_of(): return jnp.sum(lax.all_gather(local_gram, ('shard', 'tensor')), axis=0)]
    all_gather x1, waiting for transfers between devices: 24.5 us -> 14.4 us  [shards(): lax.all_gather(direction, 'shard', axis=0, tiled=True)]
  transfers between devices with their start and end apart: 9 -> 9, of which waited for: 9 -> 8; matrix products, arithmetic and copies ran while one was open for 2% -> 4% of each run, Pallas kernels for 0% -> 0%
where the time goes in v1:
time: 648 us; the launch traced here: 647 us
  waiting for transfers between devices  402 us (62%)
  blocking collectives  141 us (22%)
  matrix products  50.2 us (8%)
  other arithmetic  26.9 us (4%)
  between operations  16.7 us (3%)
  local copies, waits for them, and re-layouts  9.67 us (1%)
    all_gather x5, waiting for transfers between devices, gram_of(): return jnp.sum(lax.all_gather(local_gram, ('shard', 'tensor')), axis=0)  209 us
    reduce_scatter x1, waiting for transfers between devices, shards(): lax.psum_scatter(row_term(jnp.int32(0), lax.axis_size('shard') * rows_her...  94.5 us
    psum x1, blocking collectives, shards(): total_sq = lax.psum(square_sum, ('shard', 'tensor', 'section'))  66.8 us
    psum x1, waiting for transfers between devices, shards(): lax.psum((part_proj, gain_partial[layer_index, 0]), 'shard')  64 us
    psum x1, blocking collectives, shards(): frob = lax.psum(jnp.sum(refreshed * refreshed), ('shard', 'tensor'))  62 us
    dot_general x1, matrix products, row_term(): lax.dot_general(tokens_in, grads_out, (((0,), (0,)), ((), ())), preferred...  24.3 us
    reduce_scatter x1, waiting for transfers between devices, shards(): lax.psum_scatter(refresh_term(jnp.int32(0), lax.axis_size('tensor') * (ro...  20.4 us
    reduce_sum x5, other arithmetic, gram_of(): return jnp.sum(lax.all_gather(local_gram, ('shard', 'tensor')), axis=0)  19.7 us
  transfers between devices with their start and end apart: 9, of which 8 were waited for; matrix products, arithmetic and copies ran while one was open for 4% of the time, Pallas kernels for 0%

profile of v1, /device:TPU:1, one launch (start us, length us, event | category | flops | bytes accessed | tf_op | source)
XLA Modules:
  0.0 647.4 jit_solution(5654392718103664544)
XLA Ops:
  7.2 24.3 %fusion = f32[2048,2048]{1,0:T(8,128)} fusion(bf16[1,2048,2048]{2,1,0:T(8,128)(2,1)} %param.9, bf16[1,2048,2048]{2,1,0:T(8,128)(2,1)} %param.8), kind=kOutput, calls=%fused_computation | convolution fusion | flops 17179869184 | bytes 33554432 | tf_op jit(solution)/shard_map/dot_general | solution.py:57
  31.6 94.5 %reduce-scatter.3.cloned.1.call-done = f32[256,2048]{1,0:T(8,128)} async-done(((f32[2048,2048]{1,0:T(8,128)}), f32[256,2048]{1,0:T(8,128)}) %reduce-scatter.3.cloned.1.call-update) | async-done | bytes 2097168 | tf_op jit(solution)/shard_map/reduce_scatter | solution.py:61
  126.1 6.4 convolution_bitcast_fusion.1
  132.6 64.0 %all-reduce.2.cloned.1.call-done = f32[256,2048]{0,1:T(8,128)} async-done(((f32[256,2048]{0,1:T(8,128)}), f32[256,2048]{0,1:T(8,128)}) %all-reduce.2.cloned.1.call-update) | async-done | bytes 2097168 | tf_op jit(solution)/shard_map/psum | solution.py:68
  196.6 4.2 fusion.17
  200.9 20.4 %reduce-scatter.5.cloned.1.call-done = f32[64,256]{1,0:T(8,128)} async-done(((f32[256,256]{1,0:T(8,128)}), f32[64,256]{1,0:T(8,128)}) %reduce-scatter.5.cloned.1.call-update) | async-done | bytes 65552 | tf_op jit(solution)/shard_map/reduce_scatter | solution.py:77
  221.2 1.5 multiply_reduce_fusion.1
  222.7 62.0 %psum.31 = f32[]{:T(128)} all-reduce(f32[]{:T(128)} %multiply_reduce_fusion.1), channel_id=1, replica_groups=mesh['shard'=8,'tensor'=4,'section'=4] {'shard','tensor'}, use_global_device_ids=true, to_apply=%region_8.0 | all-reduce | flops 1 | bytes 8 | tf_op jit(solution)/shard_map/psum | solution.py:109
  285.4 2.0 fusion.14
  287.5 55.1 %all-gather.14.cloned.1.call-done = f32[8192,256]{1,0:T(8,128)} async-done(((f32[256,256]{1,0:T(8,128)}), f32[8192,256]{1,0:T(8,128)}) %all-gather.14.cloned.1.call-update) | async-done | bytes 8388624 | tf_op jit(solution)/shard_map/all_gather | solution.py:39
  342.6 4.0 reduce_sum.75
  347.2 1.1 fusion.18
  348.5 52.3 %all-gather.16.cloned.1.call-done = f32[8192,256]{1,0:T(8,128)} async-done(((f32[256,256]{1,0:T(8,128)}), f32[8192,256]{1,0:T(8,128)}) %all-gather.16.cloned.1.call-update) | async-done | bytes 8388624 | tf_op jit(solution)/shard_map/all_gather | solution.py:39
  400.8 3.9 reduce_sum.76
  405.4 1.1 fusion.19
  406.6 52.5 %all-gather.18.cloned.1.call-done = f32[8192,256]{1,0:T(8,128)} async-done(((f32[256,256]{1,0:T(8,128)}), f32[8192,256]{1,0:T(8,128)}) %all-gather.18.cloned.1.call-update) | async-done | bytes 8388624 | tf_op jit(solution)/shard_map/all_gather | solution.py:39
  459.1 3.9 reduce_sum.77
  463.7 1.1 fusion.20
  464.9 1.3 copy.20
  466.2 2.3 copy.21
  468.4 12.3 %psum.28 = f32[2048]{0:T(1024)S(1)} all-reduce(f32[2048]{0:T(1024)S(1)} %bitcast.82), channel_id=1, replica_groups=mesh['shard'=8,'tensor'=4,'section'=4] {'shard'}, use_global_device_ids=true, to_apply=%region_2.0 | all-reduce | flops 2048 | bytes 16384 | tf_op jit(solution)/shard_map/psum | solution.py:68
  482.1 1.1 multiply_reduce_fusion
  483.8 66.8 %psum.29 = f32[]{:T(128)} all-reduce(f32[]{:T(128)S(6)} %add.82), channel_id=1, replica_groups=mesh['shard'=8,'tensor'=4,'section'=4] {'shard','tensor','section'}, use_global_device_ids=true, to_apply=%region_4.0 | all-reduce | flops 1 | bytes 8 | tf_op jit(solution)/shard_map/psum | solution.py:89
  551.4 3.3 fusion.13
  554.7 2.3 copy.22
  557.3 3.9 reduce_sum.78
  561.9 1.1 fusion.21
  565.7 14.4 %all-gather.12.cloned.1.call-done = f32[256,2048]{1,0:T(8,128)} async-done(((f32[32,2048]{1,0:T(8,128)}), f32[256,2048]{1,0:T(8,128)}) %all-gather.12.cloned.1.call-update) | async-done | bytes 2097168 | tf_op jit(solution)/shard_map/all_gather | solution.py:105
  580.1 5.0 convolution_bitcast_fusion
  585.1 1.8 copy.23
  587.0 48.7 %all-gather.22.cloned.1.call-done = f32[8192,256]{1,0:T(8,128)} async-done(((f32[256,256]{1,0:T(8,128)}), f32[8192,256]{1,0:T(8,128)}) %all-gather.22.cloned.1.call-update) | async-done | bytes 8388624 | tf_op jit(solution)/shard_map/all_gather | solution.py:39
  635.7 3.9 reduce_sum.79
  (47 shorter events, 8.1 us)
Async XLA Ops:
  7.2 119.0 %copy-start = (f32[1,256,256]{2,1,0:T(8,128)S(1)}, f32[1,256,256]{2,1,0:T(8,128)}, u32[]{:S(2)}) copy-start(f32[1,256,256]{2,1,0:T(8,128)} %param.10) | copy-start | bytes 786436
  7.2 119.0 %reduce-scatter.3.cloned.1.call-start = ((), (), s32[]{:S(2)}) async-start(), calls=%async_computation.2 | async-start | bytes 18874368 | tf_op jit(solution)/shard_map/reduce_scatter | solution.py:61
  31.5 165.1 %all-reduce.2.cloned.1.call-start = ((), (), s32[]{:S(2)}) async-start(), calls=%async_computation.3 | async-start | bytes 4194304 | tf_op jit(solution)/shard_map/psum | solution.py:68
  132.5 64.1 %copy-start.1 = (f32[256,2048]{1,0:T(8,128)S(1)}, f32[256,2048]{1,0:T(8,128)}, u32[]{:S(2)}) copy-start(f32[256,2048]{1,0:T(8,128)} %reduce-scatter.3.cloned.1.call-done) | copy-start | bytes 6291460
  132.5 88.7 %reduce-scatter.5.cloned.1.call-start = ((), (), s32[]{:S(2)}) async-start(), calls=%async_computation.5 | async-start | bytes 327680 | tf_op jit(solution)/shard_map/reduce_scatter | solution.py:77
  200.8 141.7 %all-gather.14.cloned.1.call-start = ((), (), s32[]{:S(2)}) async-start(), calls=%async_computation.6 | async-start | bytes 8650752 | tf_op jit(solution)/shard_map/all_gather | solution.py:39
  287.4 113.4 %all-gather.16.cloned.1.call-start = ((), (), s32[]{:S(2)}) async-start(), calls=%async_computation.7 | async-start | bytes 8650752 | tf_op jit(solution)/shard_map/all_gather | solution.py:39
  342.6 4.4 copy-start.2
  348.3 110.8 %all-gather.18.cloned.1.call-start = ((), (), s32[]{:S(2)}) async-start(), calls=%async_computation.8 | async-start | bytes 8650752 | tf_op jit(solution)/shard_map/all_gather | solution.py:39
  406.6 150.7 %all-gather.20.cloned.1.call-start = ((), (), s32[]{:S(2)}) async-start(), calls=%async_computation.9 | async-start | bytes 8650752 | tf_op jit(solution)/shard_map/all_gather | solution.py:39
  463.0 5.4 copy-start.3
  464.8 115.3 %all-gather.12.cloned.1.call-start = ((), (), s32[]{:S(2)}) async-start(), calls=%async_computation.4 | async-start | bytes 2359296 | tf_op jit(solution)/shard_map/all_gather | solution.py:105
  557.0 78.7 %all-gather.22.cloned.1.call-start = ((), (), s32[]{:S(2)}) async-start(), calls=%async_computation.10 | async-start | bytes 8650752 | tf_op jit(solution)/shard_map/all_gather | solution.py:39
  557.3 5.8 copy-start.4
  557.3 5.8 copy-start.5
Sparse Core Ops, SparseCore 0:
  31.7 94.4 reduce-scatter.2
  132.6 63.9 all-reduce.1
  200.9 20.2 reduce-scatter.4
  287.6 54.9 all-gather.13
  348.4 52.3 all-gather.15
  406.7 52.3 all-gather.17
  464.9 52.9 all-gather.19
  557.1 22.9 all-gather.11
  582.4 53.2 all-gather.21
